TPU v7x, 128 devices: a whole 4x4x4 slice. The times are simulated.
128 devices in a mesh: aux: 4 (over x), row: 32 (over z, y, core).
Axes of the slice: x: 4, y: 4, z: 4, core: 2. Of those that a mesh axis runs over, the one named last changes fastest.
Arguments:
- b_tiles: bfloat16 [4, 32768, 2048], P('aux', 'row'), may hold values from -0.125 to 0.125
- occ_coeff: bfloat16 [32768, 256], P('row'), may hold values from -3 to 3
- tile_blocks: int32 [256, 16], P('row'), may hold values from 0 to 255, as said below
- screen_mask: int32 [256, 16], P('row'), may hold values from 0 to 1, as said below
Outputs:
- exchange: bfloat16 [32768, 32, 4, 256], P('row', None, 'aux')
Inputs may be any that keep to these rules, and one draw needn't show every extreme that they name: `tile_blocks`: each entry names a basis block at most 8 blocks away from its own row's block; the first slot of every block names the block itself. `screen_mask`: in every basis block the kept slots come first; some block keeps all 16.
All inputs are finite; a program needn't handle non-finite values.
Results may differ from a plain program's by a relative error of at most 0.0057.
Values may be sent and summed in bfloat16 or wider, within the bound.
No kernel may reach another device: no remote copies, remote signals or barrier semaphores. Data moves between devices by JAX's collectives and lax.ppermute only.
A program may use at most 128 MiB of HBM per device.

v0:
```python
import jax
import jax.numpy as jnp
from jax import lax
from jax.sharding import Mesh, PartitionSpec as P


def with_halo(block, sides, width):
    for axis, dim in sides:
        count = lax.axis_size(axis)
        forward = [(i, i + 1) for i in range(count - 1)]
        backward = [(target, source) for source, target in forward]
        low = lax.ppermute(
            lax.slice_in_dim(block, block.shape[dim] - width, None, axis=dim), axis, forward
        )
        high = lax.ppermute(lax.slice_in_dim(block, 0, width, axis=dim), axis, backward)
        block = jnp.concatenate([low, block, high], axis=dim)
    return block


ROW = ("rzy", "core")


def per_device(b_tiles, occ_coeff, tile_blocks, screen_mask):
    p_local, rows_local, stored = b_tiles.shape
    blocks_local, slot_count = tile_blocks.shape
    block_size = rows_local // blocks_local
    orbitals = occ_coeff.shape[1]
    aux_count = lax.axis_size("aux")
    row_index = lax.axis_index(ROW)
    extended = with_halo(occ_coeff, ((ROW, 0),), rows_local)
    coeff_blocks = extended.reshape(3 * blocks_local, block_size, orbitals)
    local_index = tile_blocks - (row_index - 1) * blocks_local
    picked = jnp.take(coeff_blocks, local_index, axis=0)
    keep_mask = screen_mask.astype(jnp.bfloat16)
    tiles_five = b_tiles.reshape(p_local, blocks_local, block_size, slot_count, block_size)
    masked = picked * keep_mask[:, :, None, None]
    half_sum = jnp.einsum(
        "pbmsn,bsni->pbmi", tiles_five, masked, preferred_element_type=jnp.float32
    )
    half_local = half_sum.astype(jnp.bfloat16).reshape(p_local, rows_local, orbitals)
    slab_rows = lax.all_gather(half_local, "aux", axis=0, tiled=True)
    share = rows_local // aux_count
    piece = lax.dynamic_slice_in_dim(slab_rows, lax.axis_index("aux") * share, share, axis=1)
    plane = lax.all_gather(piece, "rzy", axis=0)
    partner = lax.all_gather(plane, "core", axis=1)
    chips, cores = partner.shape[:2]
    partner = partner.reshape(chips * cores, *piece.shape)
    result = jnp.einsum("pmi,rpki->mrk", slab_rows, partner, preferred_element_type=jnp.float32)
    return result.astype(jnp.bfloat16).reshape(rows_local, chips * cores, 1, share)


def solution(mesh):
    aux_count, row_count = mesh.devices.shape
    devices = mesh.devices.reshape(aux_count, row_count // 2, 2)
    split_mesh = Mesh(devices, ("aux",) + ROW)
    in_specs = (P("aux", ROW, None), P(ROW, None), P(ROW, None), P(ROW, None))
    out_specs = P(ROW, None, "aux", None)
    return jax.shard_map(
        per_device, mesh=split_mesh, in_specs=in_specs, out_specs=out_specs, check_vma=False
    )
```

profile of v0, /device:TPU:1, one launch (start us, length us, event | category | flops | bytes accessed | tf_op | source)
XLA Modules:
  0.0 227.2 jit_solution(13417141563487165089)
XLA Ops:
  6.5 0.0 copy-start
  6.5 0.0 all-gather.6.cloned.1.call-start
  6.5 4.7 %collective-permute-start = (bf16[1024,256]{1,0:T(8,128)(2,1)}, bf16[1024,256]{1,0:T(8,128)(2,1)S(1)}, u32[]{:S(2)}, u32[]{:S(2)}) collective-permute-start(bf16[1024,256]{1,0:T(8,128)(2,1)} %param.5), channel_id=1, source_target_pairs={{0,1},{1,2},{2,3},{3,4},{4,5},{5,6},{6,7},{7,8},{8,9},{9,10},{10,1... | collective-permute-start | bytes 1572872 | tf_op jit(solution)/shard_map/ppermute | solution.py:12
  11.3 1.9 collective-permute-start.1
  13.2 0.7 convert_element_type.15
  13.9 0.7 compare_and_fusion
  14.6 0.1 reshape.32
  14.7 5.6 %copy.11 = bf16[128,8,16,128]{3,2,1,0:T(8,128)(2,1)} copy(bf16[128,8,16,128]{3,1,2,0:T(8,128)(2,1)} %bitcast.32) | data formatting | bytes 8388608
  20.2 0.0 collective-permute-done
  20.2 1.7 collective-permute-done.1
  22.0 0.0 copy-done
  22.0 0.1 pad_maximum_fusion
  22.1 6.7 %gather_fusion = bf16[128,128,256]{2,1,0:T(8,128)(2,1)} fusion(bf16[24,128,256]{2,1,0:T(8,128)(2,1)S(1)} %bitcast.29, s32[1024]{0:T(1024)S(1)} %pad_clamp_fusion), kind=kCustom, calls=%fused_computation | custom fusion | bytes 16777728 | tf_op jit(solution)/shard_map/jit(_take)/gather | solution.py:33
  28.8 8.1 %fusion.14 = bf16[8,256,128]{1,2,0:T(8,128)(2,1)} fusion(bf16[8,16,128,256]{3,2,1,0:T(8,128)(2,1)} %bitcast.30, pred[8,16]{1,0:T(8,128)(4,1)S(1)} %get-tuple-element.5, bf16[8,16]{1,0:T(8,128)(2,1)S(1)} %convert_element_type.15, bf16[8,128,16,128]{3,2,1,0:T(8,128)(2,1)} %bitcast.33), kind=kOutput, calls=%fused_computation.13 | convolution fusion | flops 1094975488 | bytes 13107584 | tf_op jit(solution)/shard_map/pbmsn,bsni->pbmi/dot_general | solution.py:37
  37.0 0.0 all-gather.6.cloned.1.call-update
  37.0 0.0 all-gather.8.cloned.1.call-start
  37.0 34.2 %all-gather.6.cloned.1.call-done = bf16[4,1024,256]{2,1,0:T(8,128)(2,1)} async-done(((bf16[1,1024,256]{2,1,0:T(8,128)(2,1)}), bf16[4,1024,256]{2,1,0:T(8,128)(2,1)}) %all-gather.6.cloned.1.call-update) | async-done | bytes 2097168 | tf_op jit(solution)/shard_map/all_gather | solution.py:41
  71.3 0.0 copy-start.1
  71.3 2.0 constant_dynamic-slice_fusion
  73.3 0.0 all-gather.8.cloned.1.call-update
  73.3 0.0 all-gather.10.cloned.1.call-start
  73.4 71.0 %all-gather.8.cloned.1.call-done = bf16[64,256,256]{2,1,0:T(8,128)(2,1)} async-done(((bf16[4,256,256]{2,1,0:T(8,128)(2,1)}), bf16[64,256,256]{2,1,0:T(8,128)(2,1)}) %all-gather.8.cloned.1.call-update) | async-done | bytes 8388624 | tf_op jit(solution)/shard_map/all_gather | solution.py:44
  144.4 0.0 all-gather.10.cloned.1.call-update
  144.4 34.5 %all-gather.10.cloned.1.call-done = bf16[16,8,256,256]{3,2,1,0:T(8,128)(2,1)} async-done(((bf16[16,4,256,256]{3,2,1,0:T(8,128)(2,1)}), bf16[16,8,256,256]{3,2,1,0:T(8,128)(2,1)}) %all-gather.10.cloned.1.call-update) | async-done | bytes 16777232 | tf_op jit(solution)/shard_map/all_gather | solution.py:45
  178.9 0.0 copy-done.1
  178.9 23.9 %fusion = bf16[1024,32,1,256]{3,0,1,2:T(8,128)(2,1)} fusion(bf16[32,4,256,256]{3,2,1,0:T(8,128)(2,1)} %bitcast.35, bf16[4,1024,256]{2,1,0:T(8,128)(2,1)S(1)} %copy-done.1), kind=kOutput, calls=%fused_computation.2 | convolution fusion | flops 17188257792 | bytes 35651584 | tf_op jit(solution)/shard_map/pmi,rpki->mrk/dot_general | solution.py:48
  202.8 17.9 %copy.8 = bf16[1024,32,1,256]{3,1,2,0:T(8,128)(2,1)} copy(bf16[1024,32,1,256]{3,0,1,2:T(8,128)(2,1)} %fusion) | data formatting | bytes 33554432 | tf_op jit(solution)/shard_map/reshape | solution.py:49
  (1 shorter events, 0.0 us)
Async XLA Ops:
  6.5 15.4 %copy-start = (bf16[1024,256]{1,0:T(8,128)(2,1)S(1)}, bf16[1024,256]{1,0:T(8,128)(2,1)}, u32[]{:S(2)}) copy-start(bf16[1024,256]{1,0:T(8,128)(2,1)} %param.5) | copy-start | bytes 1572868
  6.5 64.7 %all-gather.6.cloned.1.call-start = ((), (), s32[]{:S(2)}) async-start(), calls=%async_computation | async-start | bytes 2621440 | tf_op jit(solution)/shard_map/all_gather | solution.py:41
  6.5 13.7 %collective-permute-start = (bf16[1024,256]{1,0:T(8,128)(2,1)}, bf16[1024,256]{1,0:T(8,128)(2,1)S(1)}, u32[]{:S(2)}, u32[]{:S(2)}) collective-permute-start(bf16[1024,256]{1,0:T(8,128)(2,1)} %param.5), channel_id=1, source_target_pairs={{0,1},{1,2},{2,3},{3,4},{4,5},{5,6},{6,7},{7,8},{8,9},{9,10},{10,1... | collective-permute-start | bytes 1572872 | tf_op jit(solution)/shard_map/ppermute | solution.py:12
  11.3 10.7 %collective-permute-start.1 = (bf16[1024,256]{1,0:T(8,128)(2,1)}, bf16[1024,256]{1,0:T(8,128)(2,1)S(1)}, u32[]{:S(2)}, u32[]{:S(2)}) collective-permute-start(bf16[1024,256]{1,0:T(8,128)(2,1)} %param.5), channel_id=1, source_target_pairs={{1,0},{2,1},{3,2},{4,3},{5,4},{6,5},{7,6},{8,7},{9,8},{10,9},{11,1... | collective-permute-start | bytes 1572872 | tf_op jit(solution)/shard_map/ppermute | solution.py:15
  37.0 107.4 %all-gather.8.cloned.1.call-start = ((), (), s32[]{:S(2)}) async-start(), calls=%async_computation.1 | async-start | bytes 8912896 | tf_op jit(solution)/shard_map/all_gather | solution.py:44
  71.3 107.6 %copy-start.1 = (bf16[4,1024,256]{2,1,0:T(8,128)(2,1)S(1)}, bf16[4,1024,256]{2,1,0:T(8,128)(2,1)}, u32[]{:S(2)}) copy-start(bf16[4,1024,256]{2,1,0:T(8,128)(2,1)} %all-gather.6.cloned.1.call-done) | copy-start | bytes 6291460
  73.3 105.6 %all-gather.10.cloned.1.call-start = ((), (), s32[]{:S(2)}) async-start(), calls=%async_computation.2 | async-start | bytes 25165824 | tf_op jit(solution)/shard_map/all_gather | solution.py:45
Sparse Core Ops, SparseCore 0:
  37.1 34.1 all-gather.5
  73.4 70.8 all-gather.7
  146.1 32.7 all-gather.9
where the time goes:
time: 228 us; the launch traced here: 227 us
  waiting for transfers between devices  142 us (62%)
  local copies, waits for them, and re-layouts  32.3 us (14%)
  matrix products  32 us (14%)
  between operations  13.1 us (6%)
  starting transfers between devices  6.72 us (3%)
    all_gather x1, waiting for transfers between devices, per_device(): plane = lax.all_gather(piece, 'rzy', axis=0)  71 us
    all_gather x1, waiting for transfers between devices, per_device(): partner = lax.all_gather(plane, 'core', axis=1)  34.5 us
    all_gather x1, waiting for transfers between devices, per_device(): slab_rows = lax.all_gather(half_local, 'aux', axis=0, tiled=True)  34.2 us
    dot_general x1, matrix products, per_device(): jnp.einsum('pmi,rpki->mrk', slab_rows, partner, preferred_element_type=jn...  23.9 us
    reshape x1, local copies, waits for them, and re-layouts, per_device(): result.astype(jnp.bfloat16).reshape(rows_local, chips * cores, 1, share)  17.9 us
    dot_general x1, matrix products, per_device(): jnp.einsum('pbmsn,bsni->pbmi', tiles_five, masked, preferred_element_type...  8.14 us
    gather x1, local copies, waits for them, and re-layouts, per_device(): picked = jnp.take(coeff_blocks, local_index, axis=0)  6.75 us
    unnamed x5, local copies, waits for them, and re-layouts  5.56 us
  transfers between devices with their start and end apart: 5, of which 4 were waited for; matrix products, arithmetic and copies ran while one was open for 3% of the time, Pallas kernels for 0%

commit v1 on v0

--- a/solution.py
+++ b/solution.py
@@ -38,7 +38,14 @@
         "pbmsn,bsni->pbmi", tiles_five, masked, preferred_element_type=jnp.float32
     )
     half_local = half_sum.astype(jnp.bfloat16).reshape(p_local, rows_local, orbitals)
-    slab_rows = lax.all_gather(half_local, "aux", axis=0, tiled=True)
+    size = lax.axis_size("aux")
+    right = [(i_2, (i_2 + 1) % size) for i_2 in range(size)]
+    parts = [half_local]
+    for hop in range(1, size):
+        parts = [lax.ppermute(parts[0], "aux", right), *parts]
+    whole = jnp.concatenate(parts, axis=0)
+    shift = (lax.axis_index("aux") + 1) * parts[-1].shape[0]
+    slab_rows = jnp.roll(whole, shift, axis=0)
     share = rows_local // aux_count
     piece = lax.dynamic_slice_in_dim(slab_rows, lax.axis_index("aux") * share, share, axis=1)
     plane = lax.all_gather(piece, "rzy", axis=0)

time: 228 us -> 238 us (1.044)
  waiting for transfers between devices: 142 us -> 149 us
    ppermute x0 -> x3, waiting for transfers between devices: none -> 35.2 us  [per_device(): parts = [lax.ppermute(parts[0], 'aux', right), *parts]]
    all_gather x1 -> x0, waiting for transfers between devices: 34.2 us -> none  [per_device(): slab_rows = lax.all_gather(half_local, 'aux', axis=0, tiled=True)]
    all_gather x1, waiting for transfers between devices: 71 us -> 77.3 us  [per_device(): plane = lax.all_gather(piece, 'rzy', axis=0)]
    unnamed x5 -> x12, local copies, waits for them, and re-layouts: 5.56 us -> 7.88 us
  transfers between devices with their start and end apart: 5 -> 7, of which waited for: 4 -> 6; matrix products, arithmetic and copies ran while one was open for 3% -> 3% of each run, Pallas kernels for 0% -> 0%
where the time goes in v1:
time: 238 us; the launch traced here: 237 us
  waiting for transfers between devices  149 us (63%)
  local copies, waits for them, and re-layouts  33.5 us (14%)
  matrix products  31.4 us (13%)
  between operations  13.5 us (6%)
  starting transfers between devices  8.49 us (4%)
    all_gather x1, waiting for transfers between devices, per_device(): plane = lax.all_gather(piece, 'rzy', axis=0)  77.3 us
    ppermute x3, waiting for transfers between devices, per_device(): parts = [lax.ppermute(parts[0], 'aux', right), *parts]  35.2 us
    all_gather x1, waiting for transfers between devices, per_device(): partner = lax.all_gather(plane, 'core', axis=1)  34.5 us
    dot_general x1, matrix products, per_device(): jnp.einsum('pmi,rpki->mrk', slab_rows, partner, preferred_element_type=jn...  24.1 us
    reshape x1, local copies, waits for them, and re-layouts, per_device(): result.astype(jnp.bfloat16).reshape(rows_local, chips * cores, 1, share)  17.9 us
    unnamed x12, local copies, waits for them, and re-layouts  7.88 us
    dot_general x1, matrix products, per_device(): jnp.einsum('pbmsn,bsni->pbmi', tiles_five, masked, preferred_element_type...  7.35 us
    gather x1, local copies, waits for them, and re-layouts, per_device(): picked = jnp.take(coeff_blocks, local_index, axis=0)  6.75 us
  transfers between devices with their start and end apart: 7, of which 6 were waited for; matrix products, arithmetic and copies ran while one was open for 3% of the time, Pallas kernels for 0%

profile of v1, /device:TPU:1, one launch (start us, length us, event | category | flops | bytes accessed | tf_op | source)
XLA Modules:
  0.0 237.1 jit_solution(4242100654041030093)
XLA Ops:
  6.5 0.0 all-gather.5.cloned.1.call-start
  6.5 4.6 %collective-permute-start = (bf16[1024,256]{1,0:T(8,128)(2,1)}, bf16[1024,256]{1,0:T(8,128)(2,1)S(1)}, u32[]{:S(2)}, u32[]{:S(2)}) collective-permute-start(bf16[1024,256]{1,0:T(8,128)(2,1)} %param.5), channel_id=1, source_target_pairs={{0,1},{1,2},{2,3},{3,4},{4,5},{5,6},{6,7},{7,8},{8,9},{9,10},{10,1... | collective-permute-start | bytes 1572872 | tf_op jit(solution)/shard_map/ppermute | solution.py:12
  11.1 1.9 collective-permute-start.1
  13.1 0.7 convert_element_type.15
  13.8 0.7 compare_and_fusion
  14.5 0.1 reshape.32
  14.5 0.0 copy-start
  14.5 5.6 %copy.11 = bf16[128,8,16,128]{3,2,1,0:T(8,128)(2,1)} copy(bf16[128,8,16,128]{3,1,2,0:T(8,128)(2,1)} %bitcast.32) | data formatting | bytes 8388608
  20.2 0.0 collective-permute-done
  20.2 1.7 collective-permute-done.1
  21.8 0.0 copy-done
  21.8 0.1 pad_maximum_fusion
  22.0 6.7 %gather_fusion = bf16[128,128,256]{2,1,0:T(8,128)(2,1)} fusion(bf16[24,128,256]{2,1,0:T(8,128)(2,1)S(1)} %bitcast.29, s32[1024]{0:T(1024)S(1)} %pad_clamp_fusion), kind=kCustom, calls=%fused_computation | custom fusion | bytes 16777728 | tf_op jit(solution)/shard_map/jit(_take)/gather | solution.py:33
  28.7 7.3 %fusion.15 = bf16[8,256,128]{1,2,0:T(8,128)(2,1)S(1)} fusion(bf16[8,16,128,256]{3,2,1,0:T(8,128)(2,1)} %bitcast.30, pred[8,16]{1,0:T(8,128)(4,1)S(1)} %get-tuple-element.5, bf16[8,16]{1,0:T(8,128)(2,1)S(1)} %convert_element_type.15, bf16[8,128,16,128]{3,2,1,0:T(8,128)(2,1)} %bitcast.33), kind=kOutput, calls=%fused_computation.14 | convolution fusion | flops 1094975488 | bytes 13107584 | tf_op jit(solution)/shard_map/pbmsn,bsni->pbmi/dot_general | solution.py:37
  36.1 1.3 collective-permute-start.2
  37.3 10.0 %collective-permute-done.2 = bf16[1,1024,256]{2,1,0:T(8,128)(2,1)S(1)} collective-permute-done((bf16[1,1024,256]{2,1,0:T(8,128)(2,1)S(1)}, bf16[1,1024,256]{2,1,0:T(8,128)(2,1)S(1)}, u32[]{:S(2)}, u32[]{:S(2)}) %collective-permute-start.2) | collective-permute-done | bytes 524320 | tf_op jit(solution)/shard_map/ppermute | solution.py:45
  47.3 0.5 collective-permute-start.3
  47.8 11.8 %collective-permute-done.3 = bf16[1,1024,256]{2,1,0:T(8,128)(2,1)S(1)} collective-permute-done((bf16[1,1024,256]{2,1,0:T(8,128)(2,1)S(1)}, bf16[1,1024,256]{2,1,0:T(8,128)(2,1)S(1)}, u32[]{:S(2)}, u32[]{:S(2)}) %collective-permute-start.3) | collective-permute-done | bytes 524320 | tf_op jit(solution)/shard_map/ppermute | solution.py:45
  59.6 0.0 collective-permute-start.4
  59.6 13.4 %collective-permute-done.4 = bf16[1,1024,256]{2,1,0:T(8,128)(2,1)S(1)} collective-permute-done((bf16[1,1024,256]{2,1,0:T(8,128)(2,1)S(1)}, bf16[1,1024,256]{2,1,0:T(8,128)(2,1)S(1)}, u32[]{:S(2)}, u32[]{:S(2)}) %collective-permute-start.4) | collective-permute-done | bytes 524320 | tf_op jit(solution)/shard_map/ppermute | solution.py:45
  73.4 0.0 copy-start.1
  73.4 2.0 copy-done.1
  75.4 0.9 constant_dynamic-slice_fusion
  76.3 0.0 all-gather.5.cloned.1.call-update
  76.3 0.2 all-gather.7.cloned.1.call-start
  76.6 77.3 %all-gather.5.cloned.1.call-done = bf16[64,256,256]{2,1,0:T(8,128)(2,1)} async-done(((bf16[4,256,256]{2,1,0:T(8,128)(2,1)}), bf16[64,256,256]{2,1,0:T(8,128)(2,1)}) %all-gather.5.cloned.1.call-update) | async-done | bytes 8388624 | tf_op jit(solution)/shard_map/all_gather | solution.py:51
  153.8 0.0 all-gather.7.cloned.1.call-update
  153.8 34.5 %all-gather.7.cloned.1.call-done = bf16[16,8,256,256]{3,2,1,0:T(8,128)(2,1)} async-done(((bf16[16,4,256,256]{3,2,1,0:T(8,128)(2,1)}), bf16[16,8,256,256]{3,2,1,0:T(8,128)(2,1)}) %all-gather.7.cloned.1.call-update) | async-done | bytes 16777232 | tf_op jit(solution)/shard_map/all_gather | solution.py:52
  188.3 24.1 %fusion = bf16[1024,32,1,256]{3,0,1,2:T(8,128)(2,1)} fusion(bf16[32,4,256,256]{3,2,1,0:T(8,128)(2,1)} %bitcast.37, bf16[8,1024,256]{2,1,0:T(8,128)(2,1)} %copy-done.1, s32[]{:T(128)S(6)} %select_n.32), kind=kOutput, calls=%fused_computation.2 | convolution fusion | flops 17188257792 | bytes 35651588 | tf_op jit(solution)/shard_map/pmi,rpki->mrk/dot_general | solution.py:55
  212.4 17.9 %copy.8 = bf16[1024,32,1,256]{3,1,2,0:T(8,128)(2,1)} copy(bf16[1024,32,1,256]{3,0,1,2:T(8,128)(2,1)} %fusion) | data formatting | bytes 33554432 | tf_op jit(solution)/shard_map/reshape | solution.py:56
  (9 shorter events, 0.3 us)
Async XLA Ops:
  6.5 147.3 %all-gather.5.cloned.1.call-start = ((), (), s32[]{:S(2)}) async-start(), calls=%async_computation | async-start | bytes 8912896 | tf_op jit(solution)/shard_map/all_gather | solution.py:51
  6.5 13.6 %collective-permute-start = (bf16[1024,256]{1,0:T(8,128)(2,1)}, bf16[1024,256]{1,0:T(8,128)(2,1)S(1)}, u32[]{:S(2)}, u32[]{:S(2)}) collective-permute-start(bf16[1024,256]{1,0:T(8,128)(2,1)} %param.5), channel_id=1, source_target_pairs={{0,1},{1,2},{2,3},{3,4},{4,5},{5,6},{6,7},{7,8},{8,9},{9,10},{10,1... | collective-permute-start | bytes 1572872 | tf_op jit(solution)/shard_map/ppermute | solution.py:12
  11.1 10.7 %collective-permute-start.1 = (bf16[1024,256]{1,0:T(8,128)(2,1)}, bf16[1024,256]{1,0:T(8,128)(2,1)S(1)}, u32[]{:S(2)}, u32[]{:S(2)}) collective-permute-start(bf16[1024,256]{1,0:T(8,128)(2,1)} %param.5), channel_id=1, source_target_pairs={{1,0},{2,1},{3,2},{4,3},{5,4},{6,5},{7,6},{8,7},{9,8},{10,9},{11,1... | collective-permute-start | bytes 1572872 | tf_op jit(solution)/shard_map/ppermute | solution.py:15
  14.5 7.3 %copy-start = (bf16[1024,256]{1,0:T(8,128)(2,1)S(1)}, bf16[1024,256]{1,0:T(8,128)(2,1)}, u32[]{:S(2)}) copy-start(bf16[1024,256]{1,0:T(8,128)(2,1)} %param.5) | copy-start | bytes 1572868
  36.1 11.3 %collective-permute-start.2 = (bf16[1,1024,256]{2,1,0:T(8,128)(2,1)S(1)}, bf16[1,1024,256]{2,1,0:T(8,128)(2,1)S(1)}, u32[]{:S(2)}, u32[]{:S(2)}) collective-permute-start(bf16[1,1024,256]{2,1,0:T(8,128)(2,1)S(1)} %bitcast.34), channel_id=1, source_target_pairs={{0,32},{32,64},{64,96},{96,0},{1,33},{33,65},{65,97},{97,1},{2,34}... | collective-permute-start | bytes 1572872 | tf_op jit(solution)/shard_map/ppermute | solution.py:45
  47.3 12.3 %collective-permute-start.3 = (bf16[1,1024,256]{2,1,0:T(8,128)(2,1)S(1)}, bf16[1,1024,256]{2,1,0:T(8,128)(2,1)S(1)}, u32[]{:S(2)}, u32[]{:S(2)}) collective-permute-start(bf16[1,1024,256]{2,1,0:T(8,128)(2,1)S(1)} %collective-permute-done.2), channel_id=1, source_target_pairs={{0,32},{32,64},{64,96},{96,0},{1,33},{33,65},{65,97},{97,1},{2,34}... | collective-permute-start | bytes 1572872 | tf_op jit(solution)/shard_map/ppermute | solution.py:45
  59.6 13.4 %collective-permute-start.4 = (bf16[1,1024,256]{2,1,0:T(8,128)(2,1)S(1)}, bf16[1,1024,256]{2,1,0:T(8,128)(2,1)S(1)}, u32[]{:S(2)}, u32[]{:S(2)}) collective-permute-start(bf16[1,1024,256]{2,1,0:T(8,128)(2,1)S(1)} %collective-permute-done.3), channel_id=1, source_target_pairs={{0,32},{32,64},{64,96},{96,0},{1,33},{33,65},{65,97},{97,1},{2,34}... | collective-permute-start | bytes 1572872 | tf_op jit(solution)/shard_map/ppermute | solution.py:45
  73.4 2.0 copy-start.1
  76.3 112.0 %all-gather.7.cloned.1.call-start = ((), (), s32[]{:S(2)}) async-start(), calls=%async_computation.1 | async-start | bytes 25165824 | tf_op jit(solution)/shard_map/all_gather | solution.py:52
Sparse Core Ops, SparseCore 0:
  76.4 77.3 all-gather.4
  155.5 32.7 all-gather.6
